TPU v7x, 256 devices: a whole 4x4x8 slice. The times are simulated.
256 devices in a mesh: curve: 16 (over y, x), line: 16 (over z, core).
Axes of the slice: x: 4, y: 4, z: 8, core: 2. Of those that a mesh axis runs over, the one named last changes fastest.
Arguments:
- scaled_distributions: float32 [16, 16, 6, 27, 512], P('curve', 'line'), may hold values from 0.1 to 2.5, as said below
- remaining_brick_places: int32 [16, 16, 6], P('curve', 'line'), may hold values from -1 to 7, as said below
- retained_wavenumbers: int32 [8], replicated, may hold values from 1 to 16, as said below
- regional_amplitudes: float32 [3, 2, 512, 16], P(None, None, 'curve'), may hold values from -0.12 to 0.12
- relaxation_frequencies: float32 [27], replicated, may hold values from 0.6 to 1.8
Outputs:
- new_populations: float32 [16, 16, 6, 27, 512], P('curve', 'line')
Inputs may be any that keep to these rules, and one draw needn't show every extreme that they name: `scaled_distributions`: positive values. `remaining_brick_places`: distinct tile positions (row of the block times 4 plus its column) of one device's surviving blocks, -1 in empty slots, which may stand anywhere; at least half of each device's slots are used, and on some device all 6 are. `retained_wavenumbers`: distinct mode numbers; 16 is always among them.
All inputs are finite; a program needn't handle non-finite values.
Results may differ from a plain program's by a relative error of at most 0.0003.
Values sent between devices are 32-bit elements; how exact they have to be, the bound alone decides.
No kernel may reach another device: no remote copies, remote signals or barrier semaphores. Data moves between devices by JAX's collectives and lax.ppermute only.
A program may use at most 64 MiB of HBM per device.

v0:
```python
import jax
import jax.numpy as jnp
import numpy as np
from jax import lax
from jax.sharding import PartitionSpec as P

BE = 16
TX = 4
TY = 2
NUDGE_GAIN = 0.5
TWO_PI = 6.283185307179586
HIGHEST = lax.Precision.HIGHEST


def with_halo(block, sides, width):
    for axis, dim in sides:
        count = lax.axis_size(axis)
        forward = [(i, i + 1) for i in range(count - 1)]
        forward.append((count - 1, 0))
        backward = [(target, source) for source, target in forward]
        low = lax.ppermute(
            lax.slice_in_dim(block, block.shape[dim] - width, None, axis=dim), axis, forward
        )
        high = lax.ppermute(lax.slice_in_dim(block, 0, width, axis=dim), axis, backward)
        block = jnp.concatenate([low, block, high], axis=dim)
    return block


def lattice_tables():
    one_weights = np.array([1.0 / 6.0, 2.0 / 3.0, 1.0 / 6.0])
    speeds = np.array(
        [
            [along_x - 1, along_y - 1, along_z - 1]
            for along_x in range(3)
            for along_y in range(3)
            for along_z in range(3)
        ]
    )
    weights = np.array(
        [
            one_weights[along_x] * one_weights[along_y] * one_weights[along_z]
            for along_x in range(3)
            for along_y in range(3)
            for along_z in range(3)
        ]
    )
    vander = np.array([[1.0, 1.0, 1.0], [-1.0, 0.0, 1.0], [1.0, 0.0, 1.0]])
    undo_vander = np.array([[0.0, -0.5, 0.5], [1.0, 0.0, -1.0], [0.0, 0.5, 0.5]])
    moment_matrix = np.kron(vander, np.kron(vander, vander))
    inverse = np.kron(undo_vander, np.kron(undo_vander, undo_vander))
    forward = jnp.asarray(moment_matrix * weights[None, :], dtype=jnp.float32)
    backward = jnp.asarray(inverse / weights[:, None], dtype=jnp.float32)
    return (forward, backward, speeds)


def mode_basis_at(mode_ids, positions, length):
    phase_ids = positions[:, None] * mode_ids[None, :] % length
    angles = phase_ids.astype(jnp.float32) * (TWO_PI / length)
    return jnp.concatenate([jnp.cos(angles), jnp.sin(angles)], axis=1)


def tile_velocity(moments, safe_density):
    return jnp.stack([moments[9], moments[3], moments[1]], axis=0) / safe_density[None]


def collide_tile(moments, velocity, nudge_tile, backward, relaxation_frequencies):
    density = moments[0]
    shifted = velocity + nudge_tile
    powers = jnp.stack([jnp.ones_like(shifted), shifted, shifted * shifted + 1.0 / 3.0], axis=0)
    equilibrium = (
        density[None, None, None]
        * powers[:, None, None, 0]
        * powers[None, :, None, 1]
        * powers[None, None, :, 2]
    )
    equilibrium = equilibrium.reshape(moments.shape)
    relaxed = moments - relaxation_frequencies[:, None, None, None] * (moments - equilibrium)
    return jnp.einsum("ij,jlrc->ilrc", backward, relaxed, precision=HIGHEST)


def slot_lookup(living_brick_keys, tile_blocks):
    positions = jnp.arange(tile_blocks, dtype=jnp.int32)
    matches = living_brick_keys[None, :] == positions[:, None]
    slot_numbers = jnp.arange(living_brick_keys.shape[0], dtype=jnp.int32)
    slot_of = jnp.sum(jnp.where(matches, slot_numbers[None, :], 0), axis=1)
    present = jnp.any(matches, axis=1)
    return (slot_of, present)


def compact_to_tile(packed_arrangement, slot_of, present, rows_blocks, cols_blocks, block_edge):
    channels = packed_arrangement.shape[1]
    levels = packed_arrangement.shape[2] // (block_edge * block_edge)
    picked = jnp.take(packed_arrangement, slot_of, axis=0) * present[:, None, None].astype(
        packed_arrangement.dtype
    )
    shaped = picked.reshape(rows_blocks, cols_blocks, channels, levels, block_edge, block_edge)
    return shaped.transpose(2, 3, 0, 4, 1, 5).reshape(
        channels, levels, rows_blocks * block_edge, cols_blocks * block_edge
    )


def tile_to_compact(tile_data, living_brick_keys, rows_blocks, cols_blocks, block_edge):
    channels = tile_data.shape[0]
    levels = tile_data.shape[1]
    shaped = tile_data.reshape(
        channels, levels, rows_blocks, block_edge, cols_blocks, block_edge
    ).transpose(2, 4, 0, 1, 3, 5)
    blocks = shaped.reshape(rows_blocks * cols_blocks, channels, levels * block_edge * block_edge)
    occupied_seats = living_brick_keys >= 0
    picked = jnp.take(blocks, jnp.maximum(living_brick_keys, 0), axis=0)
    return picked * occupied_seats[:, None, None].astype(tile_data.dtype)


def on_device(
    scaled_distributions,
    remaining_brick_places,
    retained_wavenumbers,
    regional_amplitudes,
    relaxation_frequencies,
):
    forward, backward, speeds = lattice_tables()
    slot_state = scaled_distributions[0, 0]
    living_brick_keys = remaining_brick_places[0, 0]
    rows_tile = TY * BE
    cols_tile = TX * BE
    slot_of, present = slot_lookup(living_brick_keys, TX * TY)
    fluid_map = present.reshape(TY, TX).astype(jnp.float32)
    fluid_map = jnp.repeat(jnp.repeat(fluid_map, BE, axis=0), BE, axis=1)
    solid_tile = 1.0 - fluid_map
    pops_tile = compact_to_tile(slot_state, slot_of, present, TY, TX, BE)
    moments = jnp.einsum("ij,jlrc->ilrc", forward, pops_tile, precision=HIGHEST)
    safe_density = jnp.where(fluid_map[None] > 0.5, moments[0], 1.0)
    wind_tile = tile_velocity(moments, safe_density)
    line_length = lax.axis_size("line") * cols_tile
    own_columns = lax.axis_index("line") * cols_tile + jnp.arange(cols_tile, dtype=jnp.int32)
    mode_basis = mode_basis_at(retained_wavenumbers, own_columns, line_length)
    partial = jnp.einsum("klrx,xm->klrm", wind_tile, mode_basis, precision=HIGHEST)
    coefficients = lax.psum(partial, "line")
    misfit = regional_amplitudes - 2.0 / line_length * coefficients
    nudge_tile = NUDGE_GAIN * jnp.einsum("klrm,xm->klrx", misfit, mode_basis, precision=HIGHEST)
    post_tile = collide_tile(moments, wind_tile, nudge_tile, backward, relaxation_frequencies)
    levels = post_tile.shape[1]
    solid_plane = jnp.broadcast_to(solid_tile[None, None], (1, levels, rows_tile, cols_tile))
    extended = jnp.concatenate([post_tile, solid_plane], axis=0)
    padded = with_halo(extended, (("curve", 2), ("line", 3)), 1)
    pops_pad = padded[:27]
    solid_pad = padded[27, 0]
    read = []
    for discrete_heading in range(27):
        carry_eastward = int(speeds[discrete_heading, 0])
        carry_northward = int(speeds[discrete_heading, 1])
        step_z = int(speeds[discrete_heading, 2])
        rows_slice = slice(1 - carry_northward, 1 - carry_northward + rows_tile)
        cols_slice = slice(1 - carry_eastward, 1 - carry_eastward + cols_tile)
        carried_sheet = pops_pad[discrete_heading, :, rows_slice, cols_slice]
        blocked = solid_pad[rows_slice, cols_slice] > 0.5
        bounced_distributions = post_tile[26 - discrete_heading]
        if step_z == 0:
            source = carried_sheet
            block_both = jnp.stack([blocked, blocked])
        elif step_z == 1:
            source = jnp.stack([carried_sheet[0], carried_sheet[0]])
            block_both = jnp.stack([jnp.ones_like(blocked), blocked])
        else:
            mirror_sheet = pops_pad[discrete_heading + 2, 1, rows_slice, cols_slice]
            source = jnp.stack([carried_sheet[1], mirror_sheet])
            block_both = jnp.stack([blocked, blocked])
        read.append(jnp.where(block_both, bounced_distributions, source))
    read_tile = jnp.stack(read, axis=0)
    new_state = tile_to_compact(read_tile, living_brick_keys, TY, TX, BE)
    return new_state[None, None]


def solution(mesh):
    return jax.shard_map(
        on_device,
        mesh=mesh,
        in_specs=(
            P("curve", "line", None, None, None),
            P("curve", "line", None),
            P(),
            P(None, None, "curve", None),
            P(),
        ),
        out_specs=P("curve", "line", None, None, None),
        check_vma=False,
    )
```

profile of v0, /device:TPU:14, one launch (start us, length us, event | category | flops | bytes accessed | tf_op | source)
XLA Modules:
  0.0 145.7 jit_solution(17351706727084608125)
XLA Ops:
  0.0 0.8 select_reduce_fusion
  0.9 0.8 fusion.49
  4.7 1.0 copy.376
  6.9 1.0 copy.254
  8.0 2.2 %gather.13 = f32[2,4,27,2,16,16]{5,4,3,1,0,2:T(8,128)S(1)} reshape(f32[8,27,512]{2,0,1:T(8,128)} %copy.254) | data formatting | bytes 884736 | tf_op jit(solution)/shard_map/jit(_take)/gather | solution.py:93
  10.2 3.0 %multiply_bitcast_fusion = f32[27,2,2,16,4,16]{5,3,1,4,2,0:T(8,128)} fusion(f32[2,4,27,2,16,16]{5,4,3,1,0,2:T(8,128)S(1)} %gather.13, f32[2,4]{1,0:T(2,128)} %copy-done.17, pred[2,4]{1,0:T(4,128)(4,1)} %compare_and_fusion), kind=kLoop, calls=%fused_computation.2 | loop fusion | flops 221184 | bytes 884776 | tf_op jit(solution)/shard_map/transpose | solution.py:97
  13.1 3.6 %copy.255 = f32[27,2,2,16,4,16]{0,5,4,3,2,1:T(8,128)S(1)} copy(f32[27,2,2,16,4,16]{5,3,1,4,2,0:T(8,128)} %multiply_bitcast_fusion) | data formatting | bytes 884736 | tf_op jit(solution)/shard_map/transpose | solution.py:97
  17.0 5.8 %fusion.60 = f32[27,2,32,64]{3,0,2,1:T(8,128)S(1)} fusion(f32[27,27,1,1]{1,0,3,2:T(8,128)S(1)} %copy-done.15, f32[27,2,32,64]{0,3,2,1:T(8,128)S(1)} %bitcast.163), kind=kOutput, calls=%fused_computation.236 | convolution fusion | flops 35831808 | bytes 887652 | tf_op jit(solution)/shard_map/ij,jlrc->ilrc/dot_general | solution.py:131
  23.5 51.0 %psum.7 = f32[3,2,32,16]{2,3,1,0:T(8,128)S(1)} all-reduce(f32[3,2,32,16]{2,3,1,0:T(8,128)S(1)} %fusion.7), channel_id=1, replica_groups=mesh['curve'=16,'line'=16] {'line'}, use_global_device_ids=true, to_apply=%region_2.3 | all-reduce | flops 3072 | bytes 24576 | tf_op jit(solution)/shard_map/psum | solution.py:138
  75.6 1.5 %fusion.2 = f32[27,2,32,64]{3,0,2,1:T(8,128)S(1)} fusion(f32[27,27,1,1]{1,0,3,2:T(8,128)S(1)} %copy-done.14, f32[27,2,32,64]{3,0,2,1:T(8,128)S(1)} %fusion.60, f32[27,2,32,64]{3,2,1,0:T(8,128)S(1)} %bitcast.164, f32[27]{0:T(128)S(1)} %copy-done.22), kind=kOutput, calls=%fused_computation.7 | convolution fusion | flops 36163584 | bytes 1330128 | tf_op jit(solution)/shard_map/ij,jlrc->ilrc/dot_general | solution.py:78
  77.8 1.6 %collective-permute-start = (f32[28,2,1,64]{3,2,1,0:T(1,128)S(1)}, f32[28,2,1,64]{3,2,1,0:T(1,128)S(1)}, u32[]{:S(2)}, u32[]{:S(2)}) collective-permute-start(f32[28,2,1,64]{3,2,1,0:T(1,128)S(1)} %get-tuple-element.32), channel_id=1, source_target_pairs={{0,16},{16,32},{32,48},{48,64},{64,80},{80,96},{96,112},{112,128},... | collective-permute-start | bytes 43016 | tf_op jit(solution)/shard_map/ppermute | solution.py:21
  80.0 1.7 %collective-permute-done = f32[28,2,1,64]{3,2,1,0:T(1,128)S(1)} collective-permute-done((f32[28,2,1,64]{3,2,1,0:T(1,128)S(1)}, f32[28,2,1,64]{3,2,1,0:T(1,128)S(1)}, u32[]{:S(2)}, u32[]{:S(2)}) %collective-permute-start) | collective-permute-done | bytes 14368 | tf_op jit(solution)/shard_map/ppermute | solution.py:21
  81.7 3.6 %collective-permute-done.1 = f32[28,2,1,64]{3,2,1,0:T(1,128)S(1)} collective-permute-done((f32[28,2,1,64]{3,2,1,0:T(1,128)S(1)}, f32[28,2,1,64]{3,2,1,0:T(1,128)S(1)}, u32[]{:S(2)}, u32[]{:S(2)}) %collective-permute-start.1) | collective-permute-done | bytes 14368 | tf_op jit(solution)/shard_map/ppermute | solution.py:24
  88.0 0.8 stack.338
  88.7 2.7 %collective-permute-done.2 = f32[28,2,34,1]{2,1,3,0:T(2,128)S(1)} collective-permute-done((f32[28,2,34,1]{2,1,3,0:T(2,128)S(1)}, f32[28,2,34,1]{2,1,3,0:T(2,128)S(1)}, u32[]{:S(2)}, u32[]{:S(2)}) %collective-permute-start.2) | collective-permute-done | bytes 7648 | tf_op jit(solution)/shard_map/ppermute | solution.py:21
  93.3 0.8 stack.320
  94.9 0.8 stack.333
  95.7 0.8 stack.373
  96.5 0.8 stack.329
  97.4 0.8 stack.374
  98.9 0.8 stack.365
  99.6 0.8 maximum_select_fusion.3
  101.9 1.3 fusion.15
  104.1 0.8 stack.301
  104.9 0.8 stack.310
  105.9 0.8 stack.319
  106.7 0.8 stack.355
  107.6 0.8 stack.364
  108.4 0.8 stack.378
  109.2 0.8 stack.302
  109.9 0.8 stack.324
  110.7 0.8 stack.315
  112.3 0.8 stack.337
  113.0 0.8 stack.328
  114.6 0.8 stack.311
  115.4 0.8 stack.346
  116.1 0.8 stack.360
  116.9 0.8 stack.351
  117.7 0.8 stack.342
  118.5 1.0 copy_dynamic-update-slice_fusion.26
  119.5 0.9 copy_dynamic-update-slice_fusion.25
  120.4 0.9 copy_dynamic-update-slice_fusion.24
  121.3 0.9 copy_dynamic-update-slice_fusion.23
  122.2 0.9 copy_dynamic-update-slice_fusion.22
  123.1 0.9 copy_dynamic-update-slice_fusion.21
  124.0 0.9 copy_dynamic-update-slice_fusion.20
  125.0 0.9 copy_dynamic-update-slice_fusion.19
  125.9 0.9 copy_dynamic-update-slice_fusion.18
  126.8 0.9 copy_dynamic-update-slice_fusion.17
  127.7 0.9 copy_dynamic-update-slice_fusion.16
  128.6 0.9 copy_dynamic-update-slice_fusion.15
  129.6 0.9 copy_dynamic-update-slice_fusion.14
  130.5 0.9 copy_dynamic-update-slice_fusion.13
  131.5 0.9 copy_dynamic-update-slice_fusion.10
  132.4 0.9 copy_dynamic-update-slice_fusion.8
  133.4 0.9 copy_dynamic-update-slice_fusion.5
  134.3 0.9 copy_dynamic-update-slice_fusion.4
  135.2 0.9 copy_dynamic-update-slice_fusion.3
  136.2 0.9 copy_dynamic-update-slice_fusion.2
  137.1 0.9 copy_dynamic-update-slice_fusion.1
  138.0 0.9 copy_dynamic-update-slice_fusion
  138.9 3.6 %reshape.290 = f32[8,27,512]{2,0,1:T(8,128)} reshape(f32[2,4,27,2,16,16]{5,4,3,1,0,2:T(8,128)S(1)} %bitcast.165) | data formatting | bytes 884736 | tf_op jit(solution)/shard_map/reshape | solution.py:108
  142.5 1.3 copy.326
  144.6 1.1 copy.327
  (124 shorter events, 18.8 us)
Async XLA Ops:
  2.4 1.1 copy-start.17
  13.1 3.7 %copy-start.20 = (s32[8]{0:T(128)S(1)}, s32[8]{0:T(128)}, u32[]{:S(2)}) copy-start(s32[8]{0:T(128)} %param.9) | copy-start | bytes 100
  13.1 3.7 %copy-start.21 = (s32[64]{0:T(128)S(1)}, s32[64]{0:T(128)}, u32[]{:S(2)}) copy-start(s32[64]{0:T(128)} %iota_add_fusion) | copy-start | bytes 772
  13.1 3.8 %copy-start.15 = (f32[27,27,1,1]{1,0,3,2:T(8,128)S(1)}, f32[27,27,1,1]{1,0,3,2:T(8,128)}, u32[]{:S(2)}) copy-start(f32[27,27,1,1]{1,0,3,2:T(8,128)} %constant.98) | copy-start | bytes 8752
  13.1 9.6 %copy-start.16 = (pred[32,64]{1,0:T(8,128)(4,1)S(1)}, pred[32,64]{1,0:T(8,128)(4,1)}, u32[]{:S(2)}) copy-start(pred[32,64]{1,0:T(8,128)(4,1)} %copy.258) | copy-start | bytes 6148
  13.1 61.4 %copy-start.12 = (f32[3,2,32,16]{2,3,1,0:T(8,128)S(1)}, f32[3,2,32,16]{2,3,1,0:T(8,128)}, u32[]{:S(2)}) copy-start(f32[3,2,32,16]{2,3,1,0:T(8,128)} %param.10) | copy-start | bytes 36868
  16.9 58.7 %copy-start.14 = (f32[27,27,1,1]{1,0,3,2:T(8,128)S(1)}, f32[27,27,1,1]{1,0,3,2:T(8,128)}, u32[]{:S(2)}) copy-start(f32[27,27,1,1]{1,0,3,2:T(8,128)} %constant.97) | copy-start | bytes 8752
  16.9 58.7 %copy-start.22 = (f32[27]{0:T(128)S(1)}, f32[27]{0:T(128)}, u32[]{:S(2)}) copy-start(f32[27]{0:T(128)} %param.11) | copy-start | bytes 328
  77.8 3.9 %collective-permute-start = (f32[28,2,1,64]{3,2,1,0:T(1,128)S(1)}, f32[28,2,1,64]{3,2,1,0:T(1,128)S(1)}, u32[]{:S(2)}, u32[]{:S(2)}) collective-permute-start(f32[28,2,1,64]{3,2,1,0:T(1,128)S(1)} %get-tuple-element.32), channel_id=1, source_target_pairs={{0,16},{16,32},{32,48},{48,64},{64,80},{80,96},{96,112},{112,128},... | collective-permute-start | bytes 43016 | tf_op jit(solution)/shard_map/ppermute | solution.py:21
  79.3 6.0 %collective-permute-start.1 = (f32[28,2,1,64]{3,2,1,0:T(1,128)S(1)}, f32[28,2,1,64]{3,2,1,0:T(1,128)S(1)}, u32[]{:S(2)}, u32[]{:S(2)}) collective-permute-start(f32[28,2,1,64]{3,2,1,0:T(1,128)S(1)} %get-tuple-element.33), channel_id=1, source_target_pairs={{16,0},{32,16},{48,32},{64,48},{80,64},{96,80},{112,96},{128,112},... | collective-permute-start | bytes 43016 | tf_op jit(solution)/shard_map/ppermute | solution.py:24
  85.5 1.9 %copy-start.23 = (s32[1,1,6]{2,1,0:T(1,128)S(1)}, s32[1,1,6]{2,1,0:T(1,128)}, u32[]{:S(2)}) copy-start(s32[1,1,6]{2,1,0:T(1,128)} %param.8) | copy-start | bytes 76
  86.9 5.1 %collective-permute-start.3 = (f32[28,2,34,1]{2,1,3,0:T(2,128)S(1)}, f32[28,2,34,1]{2,1,3,0:T(2,128)S(1)}, u32[]{:S(2)}, u32[]{:S(2)}) collective-permute-start(f32[28,2,34,1]{2,1,3,0:T(2,128)S(1)} %copy.266), channel_id=1, source_target_pairs={{1,0},{2,1},{3,2},{4,3},{5,4},{6,5},{7,6},{8,7},{9,8},{10,9},{11,1... | collective-permute-start | bytes 22856 | tf_op jit(solution)/shard_map/ppermute | solution.py:24
  86.9 4.5 %collective-permute-start.2 = (f32[28,2,34,1]{2,1,3,0:T(2,128)S(1)}, f32[28,2,34,1]{2,1,3,0:T(2,128)S(1)}, u32[]{:S(2)}, u32[]{:S(2)}) collective-permute-start(f32[28,2,34,1]{2,1,3,0:T(2,128)S(1)} %copy.265), channel_id=1, source_target_pairs={{0,1},{1,2},{2,3},{3,4},{4,5},{5,6},{6,7},{7,8},{8,9},{9,10},{10,1... | collective-permute-start | bytes 22856 | tf_op jit(solution)/shard_map/ppermute | solution.py:21
  93.2 2.5 %copy-start.13 = (pred[32,64]{1,0:T(8,128)(4,1)}, pred[32,64]{1,0:T(8,128)(4,1)S(1)}, u32[]{:S(2)}) copy-start(pred[32,64]{1,0:T(8,128)(4,1)S(1)} %get-tuple-element.55) | copy-start | bytes 6148
  105.8 2.6 %copy-start.11 = (f32[1,32,64]{2,1,0:T(8,128)S(1)}, f32[1,32,64]{2,1,0:T(8,128)}, u32[]{:S(2)}) copy-start(f32[1,32,64]{2,1,0:T(8,128)} %get-tuple-element.5) | copy-start | bytes 24580
  105.8 4.1 %copy-start.6 = (f32[2,32,64]{2,1,0:T(8,128)S(1)}, f32[2,32,64]{2,1,0:T(8,128)}, u32[]{:S(2)}) copy-start(f32[2,32,64]{2,1,0:T(8,128)} %get-tuple-element.43) | copy-start | bytes 49156
  105.8 4.9 %copy-start.5 = (f32[2,32,64]{2,1,0:T(8,128)S(1)}, f32[2,32,64]{2,1,0:T(8,128)}, u32[]{:S(2)}) copy-start(f32[2,32,64]{2,1,0:T(8,128)} %get-tuple-element.44) | copy-start | bytes 49156
  105.8 8.7 %copy-start.10 = (f32[1,2,32,64]{3,2,1,0:T(8,128)S(1)}, f32[1,2,32,64]{3,2,1,0:T(8,128)}, u32[]{:S(2)}) copy-start(f32[1,2,32,64]{3,2,1,0:T(8,128)} %get-tuple-element.25) | copy-start | bytes 49156
  105.8 10.3 %copy-start.9 = (f32[2,32,64]{2,1,0:T(8,128)S(1)}, f32[2,32,64]{2,1,0:T(8,128)}, u32[]{:S(2)}) copy-start(f32[2,32,64]{2,1,0:T(8,128)} %get-tuple-element.38) | copy-start | bytes 49156
  105.9 11.0 %copy-start.8 = (f32[2,32,64]{2,1,0:T(8,128)S(1)}, f32[2,32,64]{2,1,0:T(8,128)}, u32[]{:S(2)}) copy-start(f32[2,32,64]{2,1,0:T(8,128)} %get-tuple-element.39) | copy-start | bytes 49156
  105.9 11.8 %copy-start.7 = (f32[2,32,64]{2,1,0:T(8,128)S(1)}, f32[2,32,64]{2,1,0:T(8,128)}, u32[]{:S(2)}) copy-start(f32[2,32,64]{2,1,0:T(8,128)} %get-tuple-element.40) | copy-start | bytes 49156
  118.5 12.9 %copy-start.4 = (f32[1,2,2,16,4,16]{5,4,3,2,1,0:T(4,128)S(1)}, f32[1,2,2,16,4,16]{5,4,3,2,1,0:T(4,128)}, u32[]{:S(2)}) copy-start(f32[1,2,2,16,4,16]{5,4,3,2,1,0:T(4,128)} %stack.342) | copy-start | bytes 49156
  118.5 13.0 %copy-start.3 = (f32[1,2,2,16,4,16]{5,4,3,2,1,0:T(4,128)S(1)}, f32[1,2,2,16,4,16]{5,4,3,2,1,0:T(4,128)}, u32[]{:S(2)}) copy-start(f32[1,2,2,16,4,16]{5,4,3,2,1,0:T(4,128)} %stack.346) | copy-start | bytes 49156
  118.5 13.9 %copy-start.2 = (f32[1,2,2,16,4,16]{5,4,3,2,1,0:T(4,128)S(1)}, f32[1,2,2,16,4,16]{5,4,3,2,1,0:T(4,128)}, u32[]{:S(2)}) copy-start(f32[1,2,2,16,4,16]{5,4,3,2,1,0:T(4,128)} %stack.351) | copy-start | bytes 49156
  118.5 14.9 %copy-start = (f32[1,2,2,16,4,16]{5,4,3,2,1,0:T(4,128)S(1)}, f32[1,2,2,16,4,16]{5,4,3,2,1,0:T(4,128)}, u32[]{:S(2)}) copy-start(f32[1,2,2,16,4,16]{5,4,3,2,1,0:T(4,128)} %stack.356) | copy-start | bytes 49156
  118.5 14.9 %copy-start.1 = (f32[1,2,2,16,4,16]{5,4,3,2,1,0:T(4,128)S(1)}, f32[1,2,2,16,4,16]{5,4,3,2,1,0:T(4,128)}, u32[]{:S(2)}) copy-start(f32[1,2,2,16,4,16]{5,4,3,2,1,0:T(4,128)} %stack.360) | copy-start | bytes 49156
  134.3 10.2 %copy-start.18 = (pred[6]{0:T(512)(128)(4,1)S(1)}, pred[6]{0:T(512)(128)(4,1)}, u32[]{:S(2)}) copy-start(pred[6]{0:T(512)(128)(4,1)} %get-tuple-element.62) | copy-start | bytes 22
  134.3 10.2 %copy-start.19 = (f32[6]{0:T(128)S(1)}, f32[6]{0:T(128)}, u32[]{:S(2)}) copy-start(f32[6]{0:T(128)} %get-tuple-element.63) | copy-start | bytes 76
where the time goes:
time: 146 us
  local copies, waits for them, and re-layouts  61 us (42%)
  blocking collectives  51 us (35%)
  other arithmetic  14.3 us (10%)
  matrix products  8.15 us (6%)
  waiting for transfers between devices  7.99 us (5%)
  starting transfers between devices  2.62 us (2%)
    psum x1, blocking collectives, on_device(): coefficients = lax.psum(partial, 'line')  51 us
    another operation x28, local copies, waits for them, and re-layouts, on_device(): read_tile = jnp.stack(read, axis=0)  21.8 us
    unnamed x75, local copies, waits for them, and re-layouts  20.5 us
    dot_general x1, matrix products, on_device(): moments = jnp.einsum('ij,jlrc->ilrc', forward, pops_tile, precision=HIGHEST)  5.79 us
    reshape x2, local copies, waits for them, and re-layouts, tile_to_compact(): shaped.reshape(rows_blocks * cols_blocks, channels, levels * block_edge *...  4.88 us
    ppermute x2, waiting for transfers between devices, with_halo(): lax.ppermute(lax.slice_in_dim(block, block.shape[dim] - width, None, axis...  4.39 us
    select_n x14, other arithmetic, on_device(): read.append(jnp.where(block_both, bounced_distributions, source))  4.2 us
    gather x3, local copies, waits for them, and re-layouts, compact_to_tile(): jnp.take(packed_arrangement, slot_of, axis=0)  3.8 us
  transfers between devices with their start and end apart: 4, of which 3 were waited for; matrix products, arithmetic and copies ran while one was open for 1% of the time, Pallas kernels for 0%

commit v1 on v0

--- a/solution.py
+++ b/solution.py
@@ -135,7 +135,7 @@
     own_columns = lax.axis_index("line") * cols_tile + jnp.arange(cols_tile, dtype=jnp.int32)
     mode_basis = mode_basis_at(retained_wavenumbers, own_columns, line_length)
     partial = jnp.einsum("klrx,xm->klrm", wind_tile, mode_basis, precision=HIGHEST)
-    coefficients = lax.psum(partial, "line")
+    coefficients = jnp.sum(lax.all_gather(partial, "line"), axis=0)
     misfit = regional_amplitudes - 2.0 / line_length * coefficients
     nudge_tile = NUDGE_GAIN * jnp.einsum("klrm,xm->klrx", misfit, mode_basis, precision=HIGHEST)
     post_tile = collide_tile(moments, wind_tile, nudge_tile, backward, relaxation_frequencies)

time: 146 us -> 118 us (0.81)
  blocking collectives: 51 us -> 22.1 us
    psum x1 -> x0, blocking collectives: 51 us -> none  [on_device(): coefficients = lax.psum(partial, 'line')]
    all_gather x0 -> x1, blocking collectives: none -> 22.1 us  [on_device(): coefficients = jnp.sum(lax.all_gather(partial, 'line'), axis=0)]
  transfers between devices with their start and end apart: 4 -> 4, of which waited for: 3 -> 3; matrix products, arithmetic and copies ran while one was open for 1% -> 2% of each run, Pallas kernels for 0% -> 0%
where the time goes in v1:
time: 118 us; the launch traced here: 117 us
  local copies, waits for them, and re-layouts  61 us (52%)
  blocking collectives  22.1 us (19%)
  other arithmetic  14.4 us (12%)
  matrix products  8.15 us (7%)
  waiting for transfers between devices  7.99 us (7%)
  starting transfers between devices  2.62 us (2%)
    all_gather x1, blocking collectives, on_device(): coefficients = jnp.sum(lax.all_gather(partial, 'line'), axis=0)  22.1 us
    another operation x28, local copies, waits for them, and re-layouts, on_device(): read_tile = jnp.stack(read, axis=0)  21.8 us
    unnamed x75, local copies, waits for them, and re-layouts  20.5 us
    dot_general x1, matrix products, on_device(): moments = jnp.einsum('ij,jlrc->ilrc', forward, pops_tile, precision=HIGHEST)  5.79 us
    reshape x2, local copies, waits for them, and re-layouts, tile_to_compact(): shaped.reshape(rows_blocks * cols_blocks, channels, levels * block_edge *...  4.88 us
    ppermute x2, waiting for transfers between devices, with_halo(): lax.ppermute(lax.slice_in_dim(block, block.shape[dim] - width, None, axis...  4.39 us
    select_n x14, other arithmetic, on_device(): read.append(jnp.where(block_both, bounced_distributions, source))  4.2 us
    gather x3, local copies, waits for them, and re-layouts, compact_to_tile(): jnp.take(packed_arrangement, slot_of, axis=0)  3.8 us
  transfers between devices with their start and end apart: 4, of which 3 were waited for; matrix products, arithmetic and copies ran while one was open for 2% of the time, Pallas kernels for 0%

profile of v1, /device:TPU:14, one launch (start us, length us, event | category | flops | bytes accessed | tf_op | source)
XLA Modules:
  0.0 116.9 jit_solution(10544610866199394814)
XLA Ops:
  0.0 0.8 select_reduce_fusion
  0.9 0.8 fusion.49
  4.7 1.0 copy.378
  6.9 1.0 copy.256
  8.0 2.2 %gather.13 = f32[2,4,27,2,16,16]{5,4,3,1,0,2:T(8,128)S(1)} reshape(f32[8,27,512]{2,0,1:T(8,128)} %copy.256) | data formatting | bytes 884736 | tf_op jit(solution)/shard_map/jit(_take)/gather | solution.py:93
  10.2 3.0 %multiply_bitcast_fusion = f32[27,2,2,16,4,16]{5,3,1,4,2,0:T(8,128)} fusion(f32[2,4,27,2,16,16]{5,4,3,1,0,2:T(8,128)S(1)} %gather.13, f32[2,4]{1,0:T(2,128)} %copy-done.17, pred[2,4]{1,0:T(4,128)(4,1)} %compare_and_fusion), kind=kLoop, calls=%fused_computation.2 | loop fusion | flops 221184 | bytes 884776 | tf_op jit(solution)/shard_map/transpose | solution.py:97
  13.1 3.6 %copy.257 = f32[27,2,2,16,4,16]{0,5,4,3,2,1:T(8,128)S(1)} copy(f32[27,2,2,16,4,16]{5,3,1,4,2,0:T(8,128)} %multiply_bitcast_fusion) | data formatting | bytes 884736 | tf_op jit(solution)/shard_map/transpose | solution.py:97
  16.9 5.8 %fusion.60 = f32[27,2,32,64]{3,0,2,1:T(8,128)S(1)} fusion(f32[27,27,1,1]{1,0,3,2:T(8,128)S(1)} %copy-done.15, f32[27,2,32,64]{0,3,2,1:T(8,128)S(1)} %bitcast.164), kind=kOutput, calls=%fused_computation.236 | convolution fusion | flops 35831808 | bytes 887652 | tf_op jit(solution)/shard_map/ij,jlrc->ilrc/dot_general | solution.py:131
  23.5 22.1 %all-gather = f32[48,2,32,16]{2,3,1,0:T(8,128)S(1)} all-gather(f32[3,2,32,16]{2,3,1,0:T(8,128)S(1)} %fusion.7), channel_id=2, replica_groups=mesh['curve'=16,'line'=16] {'line'}, dimensions={0}, use_global_device_ids=true | all-gather | bytes 208896 | tf_op jit(solution)/shard_map/all_gather | solution.py:138
  46.9 1.5 %fusion.2 = f32[27,2,32,64]{3,0,2,1:T(8,128)S(1)} fusion(f32[27,27,1,1]{1,0,3,2:T(8,128)S(1)} %copy-done.14, f32[27,2,32,64]{3,0,2,1:T(8,128)S(1)} %fusion.60, f32[27,2,32,64]{3,2,1,0:T(8,128)S(1)} %bitcast.165, f32[27]{0:T(128)S(1)} %copy-done.22), kind=kOutput, calls=%fused_computation.7 | convolution fusion | flops 36163584 | bytes 1330128 | tf_op jit(solution)/shard_map/ij,jlrc->ilrc/dot_general | solution.py:78
  49.0 1.6 %collective-permute-start = (f32[28,2,1,64]{3,2,1,0:T(1,128)S(1)}, f32[28,2,1,64]{3,2,1,0:T(1,128)S(1)}, u32[]{:S(2)}, u32[]{:S(2)}) collective-permute-start(f32[28,2,1,64]{3,2,1,0:T(1,128)S(1)} %get-tuple-element.32), channel_id=1, source_target_pairs={{0,16},{16,32},{32,48},{48,64},{64,80},{80,96},{96,112},{112,128},... | collective-permute-start | bytes 43016 | tf_op jit(solution)/shard_map/ppermute | solution.py:21
  51.2 1.7 %collective-permute-done = f32[28,2,1,64]{3,2,1,0:T(1,128)S(1)} collective-permute-done((f32[28,2,1,64]{3,2,1,0:T(1,128)S(1)}, f32[28,2,1,64]{3,2,1,0:T(1,128)S(1)}, u32[]{:S(2)}, u32[]{:S(2)}) %collective-permute-start) | collective-permute-done | bytes 14368 | tf_op jit(solution)/shard_map/ppermute | solution.py:21
  52.9 3.6 %collective-permute-done.1 = f32[28,2,1,64]{3,2,1,0:T(1,128)S(1)} collective-permute-done((f32[28,2,1,64]{3,2,1,0:T(1,128)S(1)}, f32[28,2,1,64]{3,2,1,0:T(1,128)S(1)}, u32[]{:S(2)}, u32[]{:S(2)}) %collective-permute-start.1) | collective-permute-done | bytes 14368 | tf_op jit(solution)/shard_map/ppermute | solution.py:24
  59.2 0.8 stack.338
  60.0 2.7 %collective-permute-done.2 = f32[28,2,34,1]{2,1,3,0:T(2,128)S(1)} collective-permute-done((f32[28,2,34,1]{2,1,3,0:T(2,128)S(1)}, f32[28,2,34,1]{2,1,3,0:T(2,128)S(1)}, u32[]{:S(2)}, u32[]{:S(2)}) %collective-permute-start.2) | collective-permute-done | bytes 7648 | tf_op jit(solution)/shard_map/ppermute | solution.py:21
  64.6 0.8 stack.320
  66.1 0.8 stack.333
  66.9 0.8 stack.373
  67.7 0.8 stack.329
  68.6 0.8 stack.374
  70.1 0.8 stack.365
  70.9 0.8 maximum_select_fusion.3
  73.1 1.3 %fusion.15 = (f32[2,32,64]{2,1,0:T(8,128)S(1)}, f32[2,32,64]{2,1,0:T(8,128)}, f32[2,32,64]{2,1,0:T(8,128)}, f32[2,32,64]{2,1,0:T(8,128)}) fusion(f32[27,2,32,64]{3,2,1,0:T(8,128)S(1)} %copy.266, f32[1,32,64]{2,1,0:T(8,128)S(1)} %get-tuple-element.7, pred[1,32,64]{2,1,0:T(8,128)(4,1)S(1)} %bitcast.178, f32[1,32,64]{2,1,0:T(8,128)S(1)} %get-tuple-element.6, ...), kind=kLoop, calls=%fused_computation.66 | loop fusion | flops 32768 | bytes 172032 | tf_op jit(solution)/shard_map/jit(_where)/select_n | solution.py:168
  75.3 0.8 stack.301
  76.2 0.8 stack.310
  77.1 0.8 stack.319
  78.0 0.8 stack.355
  78.8 0.8 stack.364
  79.6 0.8 stack.378
  80.4 0.8 stack.302
  81.2 0.8 stack.324
  82.0 0.8 stack.315
  83.5 0.8 stack.337
  84.3 0.8 stack.328
  85.8 0.8 stack.311
  86.6 0.8 stack.346
  87.4 0.8 stack.360
  88.1 0.8 stack.351
  88.9 0.8 stack.342
  89.7 1.0 copy_dynamic-update-slice_fusion.26
  90.7 0.9 copy_dynamic-update-slice_fusion.25
  91.6 0.9 copy_dynamic-update-slice_fusion.24
  92.5 0.9 copy_dynamic-update-slice_fusion.23
  93.4 0.9 copy_dynamic-update-slice_fusion.22
  94.4 0.9 copy_dynamic-update-slice_fusion.21
  95.3 0.9 copy_dynamic-update-slice_fusion.20
  96.2 0.9 copy_dynamic-update-slice_fusion.19
  97.1 0.9 copy_dynamic-update-slice_fusion.18
  98.0 0.9 copy_dynamic-update-slice_fusion.17
  99.0 0.9 copy_dynamic-update-slice_fusion.16
  99.9 0.9 copy_dynamic-update-slice_fusion.15
  100.8 0.9 copy_dynamic-update-slice_fusion.14
  101.7 0.9 copy_dynamic-update-slice_fusion.13
  102.7 0.9 copy_dynamic-update-slice_fusion.10
  103.6 0.9 copy_dynamic-update-slice_fusion.8
  104.6 0.9 copy_dynamic-update-slice_fusion.5
  105.5 0.9 copy_dynamic-update-slice_fusion.4
  106.5 0.9 copy_dynamic-update-slice_fusion.3
  107.4 0.9 copy_dynamic-update-slice_fusion.2
  108.3 0.9 copy_dynamic-update-slice_fusion.1
  109.2 0.9 copy_dynamic-update-slice_fusion
  110.1 3.6 %reshape.290 = f32[8,27,512]{2,0,1:T(8,128)} reshape(f32[2,4,27,2,16,16]{5,4,3,1,0,2:T(8,128)S(1)} %bitcast.166) | data formatting | bytes 884736 | tf_op jit(solution)/shard_map/reshape | solution.py:108
  113.8 1.3 %copy.328 = f32[8,27,512]{2,1,0:T(8,128)S(1)} copy(f32[8,27,512]{2,0,1:T(8,128)} %reshape.290) | data formatting | bytes 884736 | tf_op jit(solution)/shard_map/reshape | solution.py:108
  115.9 1.1 copy.329
  (125 shorter events, 18.9 us)
Async XLA Ops:
  2.4 1.1 copy-start.17
  13.1 3.6 %copy-start.20 = (s32[8]{0:T(128)S(1)}, s32[8]{0:T(128)}, u32[]{:S(2)}) copy-start(s32[8]{0:T(128)} %param.9) | copy-start | bytes 100
  13.1 3.7 %copy-start.21 = (s32[64]{0:T(128)S(1)}, s32[64]{0:T(128)}, u32[]{:S(2)}) copy-start(s32[64]{0:T(128)} %iota_add_fusion) | copy-start | bytes 772
  13.1 3.8 %copy-start.15 = (f32[27,27,1,1]{1,0,3,2:T(8,128)S(1)}, f32[27,27,1,1]{1,0,3,2:T(8,128)}, u32[]{:S(2)}) copy-start(f32[27,27,1,1]{1,0,3,2:T(8,128)} %constant.100) | copy-start | bytes 8752
  13.1 9.6 %copy-start.16 = (pred[32,64]{1,0:T(8,128)(4,1)S(1)}, pred[32,64]{1,0:T(8,128)(4,1)}, u32[]{:S(2)}) copy-start(pred[32,64]{1,0:T(8,128)(4,1)} %copy.260) | copy-start | bytes 6148
  16.8 28.9 %copy-start.12 = (f32[3,2,32,16]{2,3,1,0:T(8,128)S(1)}, f32[3,2,32,16]{2,3,1,0:T(8,128)}, u32[]{:S(2)}) copy-start(f32[3,2,32,16]{2,3,1,0:T(8,128)} %param.10) | copy-start | bytes 36868
  22.7 24.1 %copy-start.14 = (f32[27,27,1,1]{1,0,3,2:T(8,128)S(1)}, f32[27,27,1,1]{1,0,3,2:T(8,128)}, u32[]{:S(2)}) copy-start(f32[27,27,1,1]{1,0,3,2:T(8,128)} %constant.99) | copy-start | bytes 8752
  22.7 24.1 %copy-start.22 = (f32[27]{0:T(128)S(1)}, f32[27]{0:T(128)}, u32[]{:S(2)}) copy-start(f32[27]{0:T(128)} %param.11) | copy-start | bytes 328
  49.0 3.9 %collective-permute-start = (f32[28,2,1,64]{3,2,1,0:T(1,128)S(1)}, f32[28,2,1,64]{3,2,1,0:T(1,128)S(1)}, u32[]{:S(2)}, u32[]{:S(2)}) collective-permute-start(f32[28,2,1,64]{3,2,1,0:T(1,128)S(1)} %get-tuple-element.32), channel_id=1, source_target_pairs={{0,16},{16,32},{32,48},{48,64},{64,80},{80,96},{96,112},{112,128},... | collective-permute-start | bytes 43016 | tf_op jit(solution)/shard_map/ppermute | solution.py:21
  50.6 6.0 %collective-permute-start.1 = (f32[28,2,1,64]{3,2,1,0:T(1,128)S(1)}, f32[28,2,1,64]{3,2,1,0:T(1,128)S(1)}, u32[]{:S(2)}, u32[]{:S(2)}) collective-permute-start(f32[28,2,1,64]{3,2,1,0:T(1,128)S(1)} %get-tuple-element.33), channel_id=1, source_target_pairs={{16,0},{32,16},{48,32},{64,48},{80,64},{96,80},{112,96},{128,112},... | collective-permute-start | bytes 43016 | tf_op jit(solution)/shard_map/ppermute | solution.py:24
  56.7 1.9 %copy-start.23 = (s32[1,1,6]{2,1,0:T(1,128)S(1)}, s32[1,1,6]{2,1,0:T(1,128)}, u32[]{:S(2)}) copy-start(s32[1,1,6]{2,1,0:T(1,128)} %param.8) | copy-start | bytes 76
  58.1 5.1 %collective-permute-start.3 = (f32[28,2,34,1]{2,1,3,0:T(2,128)S(1)}, f32[28,2,34,1]{2,1,3,0:T(2,128)S(1)}, u32[]{:S(2)}, u32[]{:S(2)}) collective-permute-start(f32[28,2,34,1]{2,1,3,0:T(2,128)S(1)} %copy.268), channel_id=1, source_target_pairs={{1,0},{2,1},{3,2},{4,3},{5,4},{6,5},{7,6},{8,7},{9,8},{10,9},{11,1... | collective-permute-start | bytes 22856 | tf_op jit(solution)/shard_map/ppermute | solution.py:24
  58.1 4.5 %collective-permute-start.2 = (f32[28,2,34,1]{2,1,3,0:T(2,128)S(1)}, f32[28,2,34,1]{2,1,3,0:T(2,128)S(1)}, u32[]{:S(2)}, u32[]{:S(2)}) collective-permute-start(f32[28,2,34,1]{2,1,3,0:T(2,128)S(1)} %copy.267), channel_id=1, source_target_pairs={{0,1},{1,2},{2,3},{3,4},{4,5},{5,6},{6,7},{7,8},{8,9},{9,10},{10,1... | collective-permute-start | bytes 22856 | tf_op jit(solution)/shard_map/ppermute | solution.py:21
  64.4 2.5 %copy-start.13 = (pred[32,64]{1,0:T(8,128)(4,1)}, pred[32,64]{1,0:T(8,128)(4,1)S(1)}, u32[]{:S(2)}) copy-start(pred[32,64]{1,0:T(8,128)(4,1)S(1)} %get-tuple-element.55) | copy-start | bytes 6148
  77.0 2.6 %copy-start.11 = (f32[1,32,64]{2,1,0:T(8,128)S(1)}, f32[1,32,64]{2,1,0:T(8,128)}, u32[]{:S(2)}) copy-start(f32[1,32,64]{2,1,0:T(8,128)} %get-tuple-element.5) | copy-start | bytes 24580
  77.0 4.1 %copy-start.6 = (f32[2,32,64]{2,1,0:T(8,128)S(1)}, f32[2,32,64]{2,1,0:T(8,128)}, u32[]{:S(2)}) copy-start(f32[2,32,64]{2,1,0:T(8,128)} %get-tuple-element.43) | copy-start | bytes 49156
  77.1 4.9 %copy-start.5 = (f32[2,32,64]{2,1,0:T(8,128)S(1)}, f32[2,32,64]{2,1,0:T(8,128)}, u32[]{:S(2)}) copy-start(f32[2,32,64]{2,1,0:T(8,128)} %get-tuple-element.44) | copy-start | bytes 49156
  77.1 8.7 %copy-start.10 = (f32[1,2,32,64]{3,2,1,0:T(8,128)S(1)}, f32[1,2,32,64]{3,2,1,0:T(8,128)}, u32[]{:S(2)}) copy-start(f32[1,2,32,64]{3,2,1,0:T(8,128)} %get-tuple-element.25) | copy-start | bytes 49156
  77.1 10.3 %copy-start.9 = (f32[2,32,64]{2,1,0:T(8,128)S(1)}, f32[2,32,64]{2,1,0:T(8,128)}, u32[]{:S(2)}) copy-start(f32[2,32,64]{2,1,0:T(8,128)} %get-tuple-element.38) | copy-start | bytes 49156
  77.1 11.0 %copy-start.8 = (f32[2,32,64]{2,1,0:T(8,128)S(1)}, f32[2,32,64]{2,1,0:T(8,128)}, u32[]{:S(2)}) copy-start(f32[2,32,64]{2,1,0:T(8,128)} %get-tuple-element.39) | copy-start | bytes 49156
  77.1 11.8 %copy-start.7 = (f32[2,32,64]{2,1,0:T(8,128)S(1)}, f32[2,32,64]{2,1,0:T(8,128)}, u32[]{:S(2)}) copy-start(f32[2,32,64]{2,1,0:T(8,128)} %get-tuple-element.40) | copy-start | bytes 49156
  89.7 12.9 %copy-start.4 = (f32[1,2,2,16,4,16]{5,4,3,2,1,0:T(4,128)S(1)}, f32[1,2,2,16,4,16]{5,4,3,2,1,0:T(4,128)}, u32[]{:S(2)}) copy-start(f32[1,2,2,16,4,16]{5,4,3,2,1,0:T(4,128)} %stack.342) | copy-start | bytes 49156
  89.7 13.0 %copy-start.3 = (f32[1,2,2,16,4,16]{5,4,3,2,1,0:T(4,128)S(1)}, f32[1,2,2,16,4,16]{5,4,3,2,1,0:T(4,128)}, u32[]{:S(2)}) copy-start(f32[1,2,2,16,4,16]{5,4,3,2,1,0:T(4,128)} %stack.346) | copy-start | bytes 49156
  89.7 13.9 %copy-start.2 = (f32[1,2,2,16,4,16]{5,4,3,2,1,0:T(4,128)S(1)}, f32[1,2,2,16,4,16]{5,4,3,2,1,0:T(4,128)}, u32[]{:S(2)}) copy-start(f32[1,2,2,16,4,16]{5,4,3,2,1,0:T(4,128)} %stack.351) | copy-start | bytes 49156
  89.7 14.9 %copy-start = (f32[1,2,2,16,4,16]{5,4,3,2,1,0:T(4,128)S(1)}, f32[1,2,2,16,4,16]{5,4,3,2,1,0:T(4,128)}, u32[]{:S(2)}) copy-start(f32[1,2,2,16,4,16]{5,4,3,2,1,0:T(4,128)} %stack.356) | copy-start | bytes 49156
  89.7 14.9 %copy-start.1 = (f32[1,2,2,16,4,16]{5,4,3,2,1,0:T(4,128)S(1)}, f32[1,2,2,16,4,16]{5,4,3,2,1,0:T(4,128)}, u32[]{:S(2)}) copy-start(f32[1,2,2,16,4,16]{5,4,3,2,1,0:T(4,128)} %stack.360) | copy-start | bytes 49156
  105.5 10.2 %copy-start.18 = (pred[6]{0:T(512)(128)(4,1)S(1)}, pred[6]{0:T(512)(128)(4,1)}, u32[]{:S(2)}) copy-start(pred[6]{0:T(512)(128)(4,1)} %get-tuple-element.62) | copy-start | bytes 22
  105.5 10.2 %copy-start.19 = (f32[6]{0:T(128)S(1)}, f32[6]{0:T(128)}, u32[]{:S(2)}) copy-start(f32[6]{0:T(128)} %get-tuple-element.63) | copy-start | bytes 76
